TPU v7x, 32 devices: a whole 2x2x4 slice. The times are simulated.
32 devices in a mesh: expert: 8 (over z, x), tensor: 4 (over y, core).
Axes of the slice: x: 2, y: 2, z: 4, core: 2. Of those that a mesh axis runs over, the one named last changes fastest.
Arguments:
- attn_heads: bfloat16 [1024, 4096], P('expert', 'tensor'), may hold values from -6 to 6
- out_proj: bfloat16 [4096, 4096], P('tensor', 'expert'), may hold values from -0.09375 to 0.09375
- residual: bfloat16 [1024, 4096], P('expert'), may hold values from -6 to 6
- norm_gain: bfloat16 [4096], replicated, may hold values from 0.099609375 to 1.8984375
- gate_proj: bfloat16 [16, 1536, 4096], P('expert', 'tensor'), may hold values from -0.09375 to 0.09375
- up_proj: bfloat16 [16, 1536, 4096], P('expert', 'tensor'), may hold values from -0.09375 to 0.09375
- down_proj: bfloat16 [16, 1536, 4096], P('expert', None, 'tensor'), may hold values from -0.15625 to 0.15625
- expert_ids: int32 [1024, 8], P('expert'), may hold values from 0 to 15, all different within a row; in each aligned block of 128 rows (0 to 127, 128 to 255, ...) at most 96 rows name the same one
- gate_scores: float32 [1024, 8], P('expert'), may hold values from 0.25 to 1
Outputs:
- layer_out: bfloat16 [1024, 4096], P('expert', 'tensor')
Inputs may be any that keep to these rules, and one draw needn't show every extreme that they name: `expert_ids`: each row names 8 different experts. Among the 128 rows of one device no expert is named by more than 96 rows, a bound that some block reaches.
All inputs are finite; a program needn't handle non-finite values.
Results may differ from a plain program's by a relative error of at most 0.0051.
Values may be sent and summed in bfloat16 or wider, within the bound.
No kernel may reach another device: no remote copies, remote signals or barrier semaphores. Data moves between devices by JAX's collectives and lax.ppermute only.
A program may use at most 128 MiB of HBM per device.

v0:
```python
import jax
import jax.numpy as jnp
from jax import lax
from jax.sharding import PartitionSpec as P

EPS = 1e-06


def on_device(
    attn_heads,
    out_proj,
    residual,
    norm_gain,
    gate_proj,
    up_proj,
    down_proj,
    expert_ids,
    gate_scores,
):
    tok_count = residual.shape[0]
    width = residual.shape[1]
    topk = expert_ids.shape[1]
    groups = lax.axis_size("expert")
    tensor_ways = lax.axis_size("tensor")
    exp_local = gate_proj.shape[0]
    experts_all = groups * exp_local
    slot_cap = 3 * tok_count * topk // (2 * experts_all)
    share = width // tensor_ways
    offset = lax.axis_index("tensor") * share
    partial_proj = jnp.dot(
        attn_heads,
        lax.all_gather(out_proj, "expert", axis=1, tiled=True),
        preferred_element_type=jnp.float32,
    )
    attn_part = lax.psum_scatter(partial_proj, "tensor", scatter_dimension=1, tiled=True)
    res_part = lax.dynamic_slice_in_dim(residual, offset, share, 1)
    state_part = (res_part.astype(jnp.float32) + attn_part).astype(jnp.bfloat16)
    state_f = state_part.astype(jnp.float32)
    squares = lax.psum(jnp.sum(state_f * state_f, axis=1), "tensor")
    gain_part = lax.dynamic_slice_in_dim(norm_gain, offset, share, 0)
    normed = (
        state_f * lax.rsqrt(squares / width + EPS)[:, None] * gain_part.astype(jnp.float32)
    ).astype(jnp.bfloat16)
    picks = expert_ids[:, :, None] == jnp.arange(experts_all, dtype=jnp.int32)[None, None, :]
    flag = jnp.sum(picks.astype(jnp.int32), axis=1)
    before = jnp.cumsum(flag, axis=0) - flag
    rank = jnp.sum(jnp.where(picks, before[:, None, :], 0), axis=2)
    slot = expert_ids * slot_cap + rank
    token_ids = jnp.arange(tok_count * topk, dtype=jnp.int32) // topk + 1
    owner = jnp.zeros((experts_all * slot_cap,), jnp.int32).at[slot.reshape(-1)].set(token_ids)
    rows = jnp.take(normed, jnp.maximum(owner - 1, 0), axis=0)
    rows = jnp.where((owner > 0)[:, None], rows, jnp.zeros((), jnp.bfloat16))
    send = rows.reshape(groups, exp_local, slot_cap, rows.shape[1])
    block = lax.all_gather(
        lax.all_to_all(send, "expert", split_axis=0, concat_axis=0, tiled=True),
        "tensor",
        axis=3,
        tiled=True,
    )
    count = block.shape[2]
    stacked = jnp.transpose(block, (1, 0, 2, 3)).reshape(exp_local, groups * count, width)
    gate = jnp.einsum("erd,efd->erf", stacked, gate_proj, preferred_element_type=jnp.float32)
    upper = jnp.einsum("erd,efd->erf", stacked, up_proj, preferred_element_type=jnp.float32)
    act = (jax.nn.silu(gate) * upper).astype(jnp.bfloat16)
    whole_act = lax.all_gather(act, "tensor", axis=2, tiled=True)
    result = jnp.einsum(
        "erf,efd->erd", whole_act, down_proj, preferred_element_type=jnp.float32
    ).astype(jnp.bfloat16)
    result = jnp.transpose(result.reshape(exp_local, groups, count, share), (1, 0, 2, 3))
    back = lax.all_to_all(result, "expert", split_axis=0, concat_axis=0, tiled=True)
    flat = back.reshape(experts_all * slot_cap, share)
    picked = jnp.take(flat, slot.reshape(-1), axis=0).reshape(tok_count, topk, share)
    weights = gate_scores / jnp.sum(gate_scores, axis=1, keepdims=True)
    mixture = jnp.einsum("tk,tkd->td", weights, picked.astype(jnp.float32))
    return (state_part.astype(jnp.float32) + mixture).astype(jnp.bfloat16)


def solution(mesh):
    in_specs = (
        P("expert", "tensor"),
        P("tensor", "expert"),
        P("expert", None),
        P(),
        P("expert", "tensor", None),
        P("expert", "tensor", None),
        P("expert", None, "tensor"),
        P("expert", None),
        P("expert", None),
    )
    out_specs = P("expert", "tensor")
    return jax.shard_map(
        on_device, mesh=mesh, in_specs=in_specs, out_specs=out_specs, check_vma=False
    )
```

profile of v0, /device:TPU:0, one launch (start us, length us, event | category | flops | bytes accessed | tf_op | source)
XLA Modules:
  0.0 507.4 jit_solution(3773535396827234200)
XLA Ops:
  6.5 0.0 copy-start
  6.5 0.0 all-gather.4.cloned.1.call-start
  6.5 0.7 all-gather.4.cloned.1.call-update
  7.3 0.0 copy-start.4
  7.3 0.0 reduce-scatter.2.cloned.1.call-start
  7.3 130.2 %all-gather.4.cloned.1.call-done = bf16[1024,4096]{1,0:T(8,128)(2,1)} async-done(((bf16[1024,512]{1,0:T(8,128)(2,1)}), bf16[1024,4096]{1,0:T(8,128)(2,1)}) %all-gather.4.cloned.1.call-update) | async-done | bytes 8388624 | tf_op jit(solution)/shard_map/all_gather | solution.py:32
  137.5 0.0 copy-done
  137.5 6.0 %fusion.14 = f32[128,4096]{1,0:T(8,128)} fusion(bf16[128,1024]{1,0:T(8,128)(2,1)S(1)} %copy-done, bf16[1024,4096]{1,0:T(8,128)(2,1)} %all-gather.4.cloned.1.call-done), kind=kOutput, calls=%fused_computation.45 | convolution fusion | flops 1073741824 | bytes 10747904 | tf_op jit(solution)/shard_map/dot_general | solution.py:30
  143.5 0.0 reduce-scatter.2.cloned.1.call-update
  143.5 0.0 all-gather.6.cloned.1.call-start
  143.6 0.0 copy-done.4
  143.6 0.1 copy.26
  143.7 0.2 reduce_window_sum.11
  143.9 0.1 copy.28
  144.0 0.1 copy.30
  144.1 0.1 reshape.84
  144.3 4.3 scatter_custom_fusion
  148.6 0.1 broadcast_in_dim.61
  148.7 0.1 broadcast_in_dim.63
  148.8 0.7 dynamic-slice_convert_fusion
  149.5 23.8 %reduce-scatter.2.cloned.1.call-done = f32[128,1024]{1,0:T(8,128)} async-done(((f32[128,4096]{1,0:T(8,128)}), f32[128,1024]{1,0:T(8,128)}) %reduce-scatter.2.cloned.1.call-update) | async-done | bytes 524304 | tf_op jit(solution)/shard_map/reduce_scatter | solution.py:35
  173.3 1.3 fusion.3
  174.6 5.8 %psum.7 = f32[128]{0:T(128)S(1)} all-reduce(f32[128]{0:T(128)S(1)} %get-tuple-element.7), channel_id=1, replica_groups=mesh['expert'=8,'tensor'=4] {'tensor'}, use_global_device_ids=true, to_apply=%region_7.8 | all-reduce | flops 128 | bytes 1024 | tf_op jit(solution)/shard_map/psum | solution.py:39
  180.3 0.0 copy-done.2
  180.4 0.1 fusion.5
  180.5 5.1 gather_fusion
  185.6 0.6 select_select_fusion
  186.2 76.2 %all_to_all.10 = bf16[8,2,96,1024]{3,2,1,0:T(8,128)(2,1)} all-to-all(bf16[8,2,96,1024]{3,2,1,0:T(8,128)(2,1)S(1)} %select_select_fusion), channel_id=1, replica_groups=mesh['expert'=8,'tensor'=4] {'expert'}, dimensions={0} | all-to-all | bytes 6291456 | tf_op jit(solution)/shard_map/all_to_all | solution.py:55
  262.4 0.0 all-gather.6.cloned.1.call-update
  262.5 0.2 all-gather.8.cloned.1.call-start
  262.7 80.0 %all-gather.6.cloned.1.call-done = bf16[8,2,96,4096]{3,2,1,0:T(8,128)(2,1)} async-done(((bf16[8,2,96,1024]{3,2,1,0:T(8,128)(2,1)}), bf16[8,2,96,4096]{3,2,1,0:T(8,128)(2,1)}) %all-gather.6.cloned.1.call-update) | async-done | bytes 12582928 | tf_op jit(solution)/shard_map/all_gather | solution.py:54
  342.7 6.6 %copy.31 = bf16[2,8,96,4096]{3,2,1,0:T(8,128)(2,1)S(1)} copy(bf16[2,8,96,4096]{3,2,0,1:T(8,128)(2,1)} %bitcast.26) | data formatting | bytes 25165824 | tf_op jit(solution)/shard_map/transpose | solution.py:61
  349.3 0.0 slice-done
  349.3 0.0 slice-done.1
  349.3 8.1 %fusion.15 = f32[2,768,384]{2,1,0:T(8,128)} fusion(bf16[2,768,4096]{2,1,0:T(8,128)(2,1)S(1)} %bitcast.27, bf16[2,384,4096]{2,1,0:T(8,128)(2,1)S(1)} %bitcast.35), kind=kOutput, calls=%fused_computation.46 | convolution fusion | flops 4831838208 | bytes 21233664 | tf_op jit(solution)/shard_map/erd,efd->erf/dot_general | solution.py:62
  357.4 10.0 %multiply_convert_fusion = bf16[2,768,384]{2,1,0:T(8,128)(2,1)} fusion(f32[2,768,384]{2,1,0:T(8,128)} %fusion.15, bf16[2,768,4096]{2,1,0:T(8,128)(2,1)S(1)} %bitcast.28, bf16[2,384,4096]{2,1,0:T(8,128)(2,1)} %param.14), kind=kOutput, calls=%fused_computation.5 | convolution fusion | flops 4835377152 | bytes 22413312 | tf_op jit(solution)/shard_map/erd,efd->erf/dot_general | solution.py:63
  367.4 0.0 all-gather.8.cloned.1.call-update
  367.5 37.6 %all-gather.8.cloned.1.call-done = bf16[2,768,1536]{2,1,0:T(8,128)(2,1)} async-done(((bf16[2,768,384]{2,1,0:T(8,128)(2,1)}), bf16[2,768,1536]{2,1,0:T(8,128)(2,1)}) %all-gather.8.cloned.1.call-update) | async-done | bytes 4718608 | tf_op jit(solution)/shard_map/all_gather | solution.py:65
  405.0 8.6 %convolution_convert_fusion = bf16[2,768,1024]{2,1,0:T(8,128)(2,1)S(1)} fusion(bf16[2,768,1536]{2,1,0:T(8,128)(2,1)} %all-gather.8.cloned.1.call-done, bf16[2,1536,1024]{2,1,0:T(8,128)(2,1)} %param.15), kind=kOutput, calls=%fused_computation.6 | convolution fusion | flops 4833411072 | bytes 14155776 | tf_op jit(solution)/shard_map/erf,efd->erd/dot_general | solution.py:66
  413.6 1.9 copy.37
  415.5 5.6 %all-to-all-start.1 = ((bf16[8,2,96,1024]{3,2,1,0:T(8,128)(2,1)}), bf16[8,2,96,1024]{3,2,1,0:T(8,128)(2,1)S(1)}, u32[]{:S(2)}, u32[]{:S(2)}) async-start(bf16[8,2,96,1024]{3,2,1,0:T(8,128)(2,1)} %bitcast.29), calls=%async_computation.2 | async-start | bytes 6291456 | tf_op jit(solution)/shard_map/all_to_all | solution.py:70
  421.2 0.1 copy.29
  421.3 0.0 copy-done.5
  421.3 0.1 copy.33
  421.5 70.8 %all-to-all-done.1 = bf16[8,2,96,1024]{3,2,1,0:T(8,128)(2,1)S(1)} async-done(((bf16[8,2,96,1024]{3,2,1,0:T(8,128)(2,1)}), bf16[8,2,96,1024]{3,2,1,0:T(8,128)(2,1)S(1)}, u32[]{:S(2)}, u32[]{:S(2)}) %all-to-all-start.1) | async-done | bytes 3145760 | tf_op jit(solution)/shard_map/all_to_all | solution.py:70
  492.3 5.3 %gather_fusion.1 = bf16[1024,1024]{1,0:T(8,128)(2,1)} fusion(bf16[1536,1024]{1,0:T(8,128)(2,1)S(1)} %bitcast.25, s32[1024]{0:T(1024)S(1)} %broadcast_clamp_fusion), kind=kCustom, calls=%fused_computation.1 | custom fusion | bytes 4198400 | tf_op jit(solution)/shard_map/jit(_take)/gather | solution.py:72
  497.6 2.4 fusion
  500.1 0.8 fusion.6
  (22 shorter events, 0.2 us)
Async XLA Ops:
  6.5 131.0 %copy-start = (bf16[128,1024]{1,0:T(8,128)(2,1)S(1)}, bf16[128,1024]{1,0:T(8,128)(2,1)}, u32[]{:S(2)}) copy-start(bf16[128,1024]{1,0:T(8,128)(2,1)} %param.9) | copy-start | bytes 786436
  6.5 131.0 %all-gather.4.cloned.1.call-start = ((), (), s32[]{:S(2)}) async-start(), calls=%async_computation.3 | async-start | bytes 9437184 | tf_op jit(solution)/shard_map/all_gather | solution.py:32
  7.3 136.3 %copy-start.4 = (s32[128,8]{0,1:T(8,128)S(1)}, s32[128,8]{0,1:T(8,128)}, u32[]{:S(2)}) copy-start(s32[128,8]{0,1:T(8,128)} %param.16) | copy-start | bytes 12292
  7.3 166.0 %reduce-scatter.2.cloned.1.call-start = ((), (), s32[]{:S(2)}) async-start(), calls=%async_computation.4 | async-start | bytes 2621440 | tf_op jit(solution)/shard_map/reduce_scatter | solution.py:35
  143.5 199.1 %all-gather.6.cloned.1.call-start = ((), (), s32[]{:S(2)}) async-start(), calls=%async_computation.5 | async-start | bytes 15728640 | tf_op jit(solution)/shard_map/all_gather | solution.py:54
  174.6 5.8 %copy-start.2 = (bf16[128,1024]{1,0:T(8,128)(2,1)}, bf16[128,1024]{1,0:T(8,128)(2,1)S(1)}, u32[]{:S(2)}) copy-start(bf16[128,1024]{1,0:T(8,128)(2,1)S(1)} %get-tuple-element.8) | copy-start | bytes 786436
  262.4 86.8 %slice-start = ((s8[6291456]{0:T(1024)(128)(4,1)}), s8[2097152]{0:T(1024)(128)(4,1)S(1)}, s32[]{:S(2)}) async-start(s8[6291456]{0:T(1024)(128)(4,1)} %bitcast.34), calls=%async_computation.7 | async-start | bytes 4194304
  262.5 142.5 %all-gather.8.cloned.1.call-start = ((), (), s32[]{:S(2)}) async-start(), calls=%async_computation.6 | async-start | bytes 5898240 | tf_op jit(solution)/shard_map/all_gather | solution.py:65
  342.7 6.6 %slice-start.1 = ((s8[6291456]{0:T(1024)(128)(4,1)}), s8[4194304]{0:T(1024)(128)(4,1)S(1)}, s32[]{:S(2)}) async-start(s8[6291456]{0:T(1024)(128)(4,1)} %bitcast.34), calls=%async_computation.8 | async-start | bytes 8388608
  415.5 5.8 %copy-start.5 = (f32[128,8]{0,1:T(8,128)S(1)}, f32[128,8]{0,1:T(8,128)}, u32[]{:S(2)}) copy-start(f32[128,8]{0,1:T(8,128)} %param.17) | copy-start | bytes 12292
  415.5 76.8 %all-to-all-start.1 = ((bf16[8,2,96,1024]{3,2,1,0:T(8,128)(2,1)}), bf16[8,2,96,1024]{3,2,1,0:T(8,128)(2,1)S(1)}, u32[]{:S(2)}, u32[]{:S(2)}) async-start(bf16[8,2,96,1024]{3,2,1,0:T(8,128)(2,1)} %bitcast.29), calls=%async_computation.2 | async-start | bytes 6291456 | tf_op jit(solution)/shard_map/all_to_all | solution.py:70
  492.3 8.6 %copy-start.1 = (bf16[128,1024]{1,0:T(8,128)(2,1)S(1)}, bf16[128,1024]{1,0:T(8,128)(2,1)}, u32[]{:S(2)}) copy-start(bf16[128,1024]{1,0:T(8,128)(2,1)} %param.9) | copy-start | bytes 786436
  497.6 2.4 copy-start.3
Sparse Core Ops, SparseCore 0:
  9.4 128.0 all-gather.3
  143.7 29.5 reduce-scatter.1
  262.6 80.0 all-gather.5
  367.6 37.3 all-gather.7
where the time goes:
time: 508 us; the launch traced here: 507 us
  waiting for transfers between devices  343 us (68%)
  blocking collectives  82 us (16%)
  matrix products  35.1 us (7%)
  local copies, waits for them, and re-layouts  24.1 us (5%)
  between operations  13.3 us (3%)
  starting transfers between devices  5.95 us (1%)
    all_gather x1, waiting for transfers between devices, on_device(): lax.all_gather(out_proj, 'expert', axis=1, tiled=True)  130 us
    all_gather x1, waiting for transfers between devices, on_device(): lax.all_gather(lax.all_to_all(send, 'expert', split_axis=0, concat_axis=0...  80 us
    all_to_all x1, blocking collectives, on_device(): lax.all_to_all(send, 'expert', split_axis=0, concat_axis=0, tiled=True)  76.2 us
    all_to_all x1, waiting for transfers between devices, on_device(): lax.all_to_all(result, 'expert', split_axis=0, concat_axis=0, tiled=True)  70.8 us
    all_gather x1, waiting for transfers between devices, on_device(): whole_act = lax.all_gather(act, 'tensor', axis=2, tiled=True)  37.6 us
    reduce_scatter x1, waiting for transfers between devices, on_device(): lax.psum_scatter(partial_proj, 'tensor', scatter_dimension=1, tiled=True)  23.8 us
  transfers between devices with their start and end apart: 5, of which 5 were waited for; matrix products, arithmetic and copies ran while one was open for 1% of the time, Pallas kernels for 0%

commit v1 on v0

--- a/solution.py
+++ b/solution.py
@@ -62,7 +62,13 @@
     gate = jnp.einsum("erd,efd->erf", stacked, gate_proj, preferred_element_type=jnp.float32)
     upper = jnp.einsum("erd,efd->erf", stacked, up_proj, preferred_element_type=jnp.float32)
     act = (jax.nn.silu(gate) * upper).astype(jnp.bfloat16)
-    whole_act = lax.all_gather(act, "tensor", axis=2, tiled=True)
+    devices = lax.axis_size("tensor")
+    block_2, tiles = (act, [act])
+    for _ in range(devices - 1):
+        block_2 = lax.ppermute(block_2, "tensor", [(i, (i + 1) % devices) for i in range(devices)])
+        tiles.insert(0, block_2)
+    row_of_blocks = jnp.concatenate(tiles, axis=2)
+    whole_act = jnp.roll(row_of_blocks, (lax.axis_index("tensor") + 1) * act.shape[2], axis=2)
     result = jnp.einsum(
         "erf,efd->erd", whole_act, down_proj, preferred_element_type=jnp.float32
     ).astype(jnp.bfloat16)

time: 508 us -> 535 us (1.053)
  local copies, waits for them, and re-layouts: 24.1 us -> 34.2 us
  matrix products: 35.1 us -> 43.5 us
  waiting for transfers between devices: 343 us -> 351 us
    ppermute x0 -> x3, waiting for transfers between devices: none -> 47 us  [on_device(): lax.ppermute(block_2, 'tensor', [(i, (i + 1) % devices) for i in range(de...]
    all_gather x1 -> x0, waiting for transfers between devices: 37.6 us -> none  [on_device(): whole_act = lax.all_gather(act, 'tensor', axis=2, tiled=True)]
    dot_general x1, matrix products: 8.07 us -> 15 us  [on_device(): jnp.einsum('erd,efd->erf', stacked, gate_proj, preferred_element_type=jnp...]
    unnamed x16 -> x21, local copies, waits for them, and re-layouts: 0.03 us -> 5.96 us
  transfers between devices with their start and end apart: 5 -> 7, of which waited for: 5 -> 7; matrix products, arithmetic and copies ran while one was open for 1% -> 1% of each run, Pallas kernels for 0% -> 0%
where the time goes in v1:
time: 535 us
  waiting for transfers between devices  351 us (66%)
  blocking collectives  82 us (15%)
  matrix products  43.5 us (8%)
  local copies, waits for them, and re-layouts  34.2 us (6%)
  between operations  13.3 us (2%)
  starting transfers between devices  6.05 us (1%)
    all_gather x1, waiting for transfers between devices, on_device(): lax.all_gather(out_proj, 'expert', axis=1, tiled=True)  130 us
    all_gather x1, waiting for transfers between devices, on_device(): lax.all_gather(lax.all_to_all(send, 'expert', split_axis=0, concat_axis=0...  80.2 us
    all_to_all x1, blocking collectives, on_device(): lax.all_to_all(send, 'expert', split_axis=0, concat_axis=0, tiled=True)  76.2 us
    all_to_all x1, waiting for transfers between devices, on_device(): lax.all_to_all(result, 'expert', split_axis=0, concat_axis=0, tiled=True)  68.8 us
    ppermute x3, waiting for transfers between devices, on_device(): lax.ppermute(block_2, 'tensor', [(i, (i + 1) % devices) for i in range(de...  47 us
    reduce_scatter x1, waiting for transfers between devices, on_device(): lax.psum_scatter(partial_proj, 'tensor', scatter_dimension=1, tiled=True)  23.8 us
    dot_general x1, matrix products, on_device(): jnp.einsum('erd,efd->erf', stacked, gate_proj, preferred_element_type=jnp...  15 us
    dot_general x1, matrix products, on_device(): jnp.einsum('erd,efd->erf', stacked, up_proj, preferred_element_type=jnp.f...  14.5 us
  transfers between devices with their start and end apart: 7, of which 7 were waited for; matrix products, arithmetic and copies ran while one was open for 1% of the time, Pallas kernels for 0%

profile of v1, /device:TPU:0, one launch (start us, length us, event | category | flops | bytes accessed | tf_op | source)
XLA Modules:
  0.0 534.7 jit_solution(15912184411036667015)
XLA Ops:
  6.5 0.7 all-gather.3.cloned.1.call-update
  7.3 0.0 reduce-scatter.2.cloned.1.call-start
  7.3 130.2 %all-gather.3.cloned.1.call-done = bf16[1024,4096]{1,0:T(8,128)(2,1)} async-done(((bf16[1024,512]{1,0:T(8,128)(2,1)}), bf16[1024,4096]{1,0:T(8,128)(2,1)}) %all-gather.3.cloned.1.call-update) | async-done | bytes 8388624 | tf_op jit(solution)/shard_map/all_gather | solution.py:32
  137.5 6.0 %fusion.20 = f32[128,4096]{1,0:T(8,128)} fusion(bf16[128,1024]{1,0:T(8,128)(2,1)S(1)} %copy-done, bf16[1024,4096]{1,0:T(8,128)(2,1)} %all-gather.3.cloned.1.call-done), kind=kOutput, calls=%fused_computation.56 | convolution fusion | flops 1073741824 | bytes 10747904 | tf_op jit(solution)/shard_map/dot_general | solution.py:30
  143.5 0.0 reduce-scatter.2.cloned.1.call-update
  143.6 0.0 all-gather.5.cloned.1.call-start
  143.6 0.1 copy.29
  143.7 0.2 reduce_window_sum.11
  143.9 0.1 copy.31
  144.0 0.1 copy.33
  144.1 0.1 reshape.84
  144.3 4.3 scatter_custom_fusion
  148.6 0.1 broadcast_in_dim.61
  148.7 0.1 broadcast_in_dim.63
  148.8 0.7 dynamic-slice_convert_fusion
  149.5 23.8 %reduce-scatter.2.cloned.1.call-done = f32[128,1024]{1,0:T(8,128)} async-done(((f32[128,4096]{1,0:T(8,128)}), f32[128,1024]{1,0:T(8,128)}) %reduce-scatter.2.cloned.1.call-update) | async-done | bytes 524304 | tf_op jit(solution)/shard_map/reduce_scatter | solution.py:35
  173.3 1.3 fusion.8
  174.6 5.8 %psum.7 = f32[128]{0:T(128)S(1)} all-reduce(f32[128]{0:T(128)S(1)} %get-tuple-element.7), channel_id=1, replica_groups=mesh['expert'=8,'tensor'=4] {'tensor'}, use_global_device_ids=true, to_apply=%region_7.8 | all-reduce | flops 128 | bytes 1024 | tf_op jit(solution)/shard_map/psum | solution.py:39
  180.4 0.1 fusion.10
  180.5 5.1 gather_fusion
  185.6 0.6 select_select_fusion
  186.2 76.2 %all_to_all.10 = bf16[8,2,96,1024]{3,2,1,0:T(8,128)(2,1)} all-to-all(bf16[8,2,96,1024]{3,2,1,0:T(8,128)(2,1)S(1)} %select_select_fusion), channel_id=1, replica_groups=mesh['expert'=8,'tensor'=4] {'expert'}, dimensions={0} | all-to-all | bytes 6291456 | tf_op jit(solution)/shard_map/all_to_all | solution.py:55
  262.4 0.0 all-gather.5.cloned.1.call-update
  262.5 80.2 %all-gather.5.cloned.1.call-done = bf16[8,2,96,4096]{3,2,1,0:T(8,128)(2,1)} async-done(((bf16[8,2,96,1024]{3,2,1,0:T(8,128)(2,1)}), bf16[8,2,96,4096]{3,2,1,0:T(8,128)(2,1)}) %all-gather.5.cloned.1.call-update) | async-done | bytes 12582928 | tf_op jit(solution)/shard_map/all_gather | solution.py:54
  342.7 10.7 %copy.34 = bf16[2,8,96,4096]{3,2,1,0:T(8,128)(2,1)} copy(bf16[2,8,96,4096]{3,2,0,1:T(8,128)(2,1)} %bitcast.25) | data formatting | bytes 25165824 | tf_op jit(solution)/shard_map/transpose | solution.py:61
  353.3 15.0 %fusion.21 = f32[2,768,384]{1,2,0:T(8,128)} fusion(bf16[2,768,4096]{2,1,0:T(8,128)(2,1)} %bitcast.26, bf16[2,384,4096]{2,1,0:T(8,128)(2,1)} %param.13), kind=kOutput, calls=%fused_computation.57 | convolution fusion | flops 4831838208 | bytes 21233664 | tf_op jit(solution)/shard_map/erd,efd->erf/dot_general | solution.py:62
  368.4 14.5 %multiply_convert_fusion = bf16[2,768,384]{1,2,0:T(8,128)(2,1)S(1)} fusion(f32[2,768,384]{1,2,0:T(8,128)} %fusion.21, bf16[2,768,4096]{2,1,0:T(8,128)(2,1)} %bitcast.27, bf16[2,384,4096]{2,1,0:T(8,128)(2,1)} %param.14), kind=kOutput, calls=%fused_computation.7 | convolution fusion | flops 4835377152 | bytes 22413312 | tf_op jit(solution)/shard_map/erd,efd->erf/dot_general | solution.py:63
  382.9 0.3 collective-permute-start
  383.2 15.4 %collective-permute-done = bf16[2,768,384]{1,2,0:T(8,128)(2,1)S(1)} collective-permute-done((bf16[2,768,384]{1,2,0:T(8,128)(2,1)S(1)}, bf16[2,768,384]{1,2,0:T(8,128)(2,1)S(1)}, u32[]{:S(2)}, u32[]{:S(2)}) %collective-permute-start) | collective-permute-done | bytes 1179680 | tf_op jit(solution)/shard_map/ppermute | solution.py:68
  398.6 15.7 %collective-permute-done.1 = bf16[2,768,384]{1,2,0:T(8,128)(2,1)} collective-permute-done((bf16[2,768,384]{1,2,0:T(8,128)(2,1)S(1)}, bf16[2,768,384]{1,2,0:T(8,128)(2,1)}, u32[]{:S(2)}, u32[]{:S(2)}) %collective-permute-start.1) | collective-permute-done | bytes 1179680 | tf_op jit(solution)/shard_map/ppermute | solution.py:68
  414.3 15.9 %collective-permute-done.2 = bf16[2,768,384]{1,2,0:T(8,128)(2,1)} collective-permute-done((bf16[2,768,384]{1,2,0:T(8,128)(2,1)}, bf16[2,768,384]{1,2,0:T(8,128)(2,1)}, u32[]{:S(2)}, u32[]{:S(2)}) %collective-permute-start.2) | collective-permute-done | bytes 1179680 | tf_op jit(solution)/shard_map/ppermute | solution.py:68
  430.3 1.3 constant_dynamic-update-slice_fusion.7
  431.6 1.5 constant_dynamic-update-slice_fusion.6
  433.1 0.1 constant_dynamic-update-slice_fusion.5
  433.2 0.1 constant_dynamic-update-slice_fusion.4
  433.3 1.5 constant_dynamic-update-slice_fusion.3
  434.8 1.3 constant_dynamic-update-slice_fusion.2
  436.2 0.1 constant_dynamic-update-slice_fusion.1
  436.3 0.1 constant_dynamic-update-slice_fusion
  436.4 5.6 %fusion.2 = bf16[2,768,1024]{2,1,0:T(8,128)(2,1)S(1)} fusion(bf16[2,1536,1024]{2,1,0:T(8,128)(2,1)S(1)} %bitcast.34, bf16[2,768,3072]{1,2,0:T(8,128)(2,1)S(1)} %constant_dynamic-update-slice_fusion, s32[]{:T(128)S(6)} %select_n.69), kind=kOutput, calls=%fused_computation.8 | convolution fusion | flops 4833411072 | bytes 14155780 | tf_op jit(solution)/shard_map/erf,efd->erd/dot_general | solution.py:72
  441.9 2.0 copy.42
  443.9 5.6 %all-to-all-start.1 = ((bf16[8,2,96,1024]{3,2,1,0:T(8,128)(2,1)}), bf16[8,2,96,1024]{3,2,1,0:T(8,128)(2,1)S(1)}, u32[]{:S(2)}, u32[]{:S(2)}) async-start(bf16[8,2,96,1024]{3,2,1,0:T(8,128)(2,1)} %bitcast.28), calls=%async_computation.2 | async-start | bytes 6291456 | tf_op jit(solution)/shard_map/all_to_all | solution.py:76
  449.6 0.1 copy.32
  449.7 0.1 copy.38
  449.9 68.8 %all-to-all-done.1 = bf16[8,2,96,1024]{3,2,1,0:T(8,128)(2,1)S(1)} async-done(((bf16[8,2,96,1024]{3,2,1,0:T(8,128)(2,1)}), bf16[8,2,96,1024]{3,2,1,0:T(8,128)(2,1)S(1)}, u32[]{:S(2)}, u32[]{:S(2)}) %all-to-all-start.1) | async-done | bytes 3145760 | tf_op jit(solution)/shard_map/all_to_all | solution.py:76
  518.6 5.3 gather_fusion.1
  524.0 2.4 fusion.5
  526.4 1.8 fusion.11
  (31 shorter events, 0.2 us)
Async XLA Ops:
  6.5 131.0 %copy-start = (bf16[128,1024]{1,0:T(8,128)(2,1)S(1)}, bf16[128,1024]{1,0:T(8,128)(2,1)}, u32[]{:S(2)}) copy-start(bf16[128,1024]{1,0:T(8,128)(2,1)} %param.9) | copy-start | bytes 786436
  6.5 131.0 %all-gather.3.cloned.1.call-start = ((), (), s32[]{:S(2)}) async-start(), calls=%async_computation.3 | async-start | bytes 9437184 | tf_op jit(solution)/shard_map/all_gather | solution.py:32
  7.3 136.4 %copy-start.3 = (s32[128,8]{0,1:T(8,128)S(1)}, s32[128,8]{0,1:T(8,128)}, u32[]{:S(2)}) copy-start(s32[128,8]{0,1:T(8,128)} %param.16) | copy-start | bytes 12292
  7.3 166.0 %reduce-scatter.2.cloned.1.call-start = ((), (), s32[]{:S(2)}) async-start(), calls=%async_computation.4 | async-start | bytes 2621440 | tf_op jit(solution)/shard_map/reduce_scatter | solution.py:35
  143.6 199.1 %all-gather.5.cloned.1.call-start = ((), (), s32[]{:S(2)}) async-start(), calls=%async_computation.5 | async-start | bytes 15728640 | tf_op jit(solution)/shard_map/all_gather | solution.py:54
  174.6 5.8 %copy-start.2 = (bf16[128,1024]{1,0:T(8,128)(2,1)}, bf16[128,1024]{1,0:T(8,128)(2,1)S(1)}, u32[]{:S(2)}) copy-start(bf16[128,1024]{1,0:T(8,128)(2,1)S(1)} %get-tuple-element.8) | copy-start | bytes 786436
  382.9 15.7 %collective-permute-start = (bf16[2,768,384]{1,2,0:T(8,128)(2,1)S(1)}, bf16[2,768,384]{1,2,0:T(8,128)(2,1)S(1)}, u32[]{:S(2)}, u32[]{:S(2)}) collective-permute-start(bf16[2,768,384]{1,2,0:T(8,128)(2,1)S(1)} %multiply_convert_fusion), channel_id=1, source_target_pairs={{0,1},{1,2},{2,3},{3,0},{4,5},{5,6},{6,7},{7,4},{8,9},{9,10},{10,1... | collective-permute-start | bytes 3538952 | tf_op jit(solution)/shard_map/ppermute | solution.py:68
  398.6 15.7 %collective-permute-start.1 = (bf16[2,768,384]{1,2,0:T(8,128)(2,1)S(1)}, bf16[2,768,384]{1,2,0:T(8,128)(2,1)}, u32[]{:S(2)}, u32[]{:S(2)}) collective-permute-start(bf16[2,768,384]{1,2,0:T(8,128)(2,1)S(1)} %collective-permute-done), channel_id=1, source_target_pairs={{0,1},{1,2},{2,3},{3,0},{4,5},{5,6},{6,7},{7,4},{8,9},{9,10},{10,1... | collective-permute-start | bytes 3538952 | tf_op jit(solution)/shard_map/ppermute | solution.py:68
  414.3 15.9 %collective-permute-start.2 = (bf16[2,768,384]{1,2,0:T(8,128)(2,1)}, bf16[2,768,384]{1,2,0:T(8,128)(2,1)}, u32[]{:S(2)}, u32[]{:S(2)}) collective-permute-start(bf16[2,768,384]{1,2,0:T(8,128)(2,1)} %collective-permute-done.1), channel_id=1, source_target_pairs={{0,1},{1,2},{2,3},{3,0},{4,5},{5,6},{6,7},{7,4},{8,9},{9,10},{10,1... | collective-permute-start | bytes 3538952 | tf_op jit(solution)/shard_map/ppermute | solution.py:68
  431.6 4.7 slice-start
  433.3 3.1 slice-start.1
  443.9 5.8 %copy-start.4 = (f32[128,8]{0,1:T(8,128)S(1)}, f32[128,8]{0,1:T(8,128)}, u32[]{:S(2)}) copy-start(f32[128,8]{0,1:T(8,128)} %param.17) | copy-start | bytes 12292
  443.9 74.7 %all-to-all-start.1 = ((bf16[8,2,96,1024]{3,2,1,0:T(8,128)(2,1)}), bf16[8,2,96,1024]{3,2,1,0:T(8,128)(2,1)S(1)}, u32[]{:S(2)}, u32[]{:S(2)}) async-start(bf16[8,2,96,1024]{3,2,1,0:T(8,128)(2,1)} %bitcast.28), calls=%async_computation.2 | async-start | bytes 6291456 | tf_op jit(solution)/shard_map/all_to_all | solution.py:76
  518.6 9.5 %copy-start.1 = (bf16[128,1024]{1,0:T(8,128)(2,1)S(1)}, bf16[128,1024]{1,0:T(8,128)(2,1)}, u32[]{:S(2)}) copy-start(bf16[128,1024]{1,0:T(8,128)(2,1)} %param.9) | copy-start | bytes 786436
Sparse Core Ops, SparseCore 0:
  9.4 128.0 all-gather.2
  143.7 29.5 reduce-scatter.1
  262.6 80.0 all-gather.4
